TPU v7x, 512 devices: a whole 4x8x8 slice. The times are simulated.
512 devices in a mesh: dp: 64 (over z, y), seq: 8 (over x, core).
Axes of the slice: x: 4, y: 8, z: 8, core: 2. Of those that a mesh axis runs over, the one named last changes fastest.
Arguments:
- checkpoint: bfloat16 [65536, 8192], P(('dp', 'seq')), may hold values from -6 to 6
- norm_gain: float32 [8192], replicated, may hold values from 0.1 to 1.9
- key_cotangent: bfloat16 [65536, 1024], P(('dp', 'seq')), may hold values from -6 to 6
- positions: int32 [65536], P(('dp', 'seq')), may hold values from 0 to 4095, as said below
- kept_cols: int32 [128, 6], replicated, may hold values from 0 to 15, as said below
- kept_count: int32 [128], replicated, may hold values from 2 to 6
- key_blocks: bfloat16 [128, 6, 4096], P('dp'), may hold values from -0.375 to 0.375
Outputs:
- input_grad: bfloat16 [65536, 8192], P(('dp', 'seq'))
- block_grad: float32 [128, 6, 4096], P('dp', None, 'seq')
Inputs may be any that keep to these rules, and one draw needn't show every extreme that they name: `kept_cols`: the 6 entries of a row are different block columns; only the first kept_count entries of a row name kept blocks, the others are unused slots. Inside a document the positions rise by one from token to token.
All inputs are finite; a program needn't handle non-finite values.
Results may differ from a plain program's by a relative error of at most 0.0049.
Values may be sent and summed in bfloat16 or wider, within the bound.
No kernel may reach another device: no remote copies, remote signals or barrier semaphores. Data moves between devices by JAX's collectives and lax.ppermute only.
A program may use at most 128 MiB of HBM per device.

v0:
```python
import math
import jax
import jax.numpy as jnp
from jax import lax
from jax.sharding import PartitionSpec as P

D = 8192
KVW = 1024
HEAD_DIM = 128
BLK = 64
MOSTR = 6
SEQ_LEN = 1024


def rope_back(grad, positions):
    heads = KVW // HEAD_DIM
    half = HEAD_DIM // 2
    values = grad.astype(jnp.float32).reshape(-1, heads, 2, half)
    freqs = 10000.0 ** (-2.0 * jnp.arange(half).astype(jnp.float32) / HEAD_DIM)
    angle = positions.astype(jnp.float32)[:, None] * freqs[None, :]
    cosine = jnp.cos(angle)[:, None, :]
    sine = jnp.sin(angle)[:, None, :]
    first = values[:, :, 0] * cosine + values[:, :, 1] * sine
    second = values[:, :, 1] * cosine - values[:, :, 0] * sine
    return jnp.stack([first, second], axis=2).reshape(-1, KVW).astype(jnp.bfloat16)


def densify(blocks, cols, count, rows):
    count_rows = blocks.shape[0]
    col_blocks = KVW // BLK
    slot_ids = lax.broadcasted_iota(jnp.int32, (count_rows, MOSTR), 1)
    live = slot_ids < count[:, None]
    col_ids = lax.broadcasted_iota(jnp.int32, (count_rows, MOSTR, col_blocks), 2)
    onehot = ((cols[:, :, None] == col_ids) & live[:, :, None]).astype(jnp.bfloat16)
    placed = lax.dot_general(
        onehot, blocks, (((1,), (1,)), ((0,), (0,))), preferred_element_type=jnp.bfloat16
    )
    dense = placed.reshape(count_rows, col_blocks, rows, BLK).transpose(0, 2, 1, 3)
    return dense.reshape(count_rows * rows, KVW)


def shards(checkpoint, norm_gain, key_cotangent, positions, kept_cols, kept_count, key_blocks):
    tok_rows = checkpoint.shape[0]
    groups = lax.axis_size("seq")
    part_rows = BLK // groups
    row_blocks = D // BLK
    col_blocks = KVW // BLK
    xf = checkpoint.astype(jnp.float32)
    inv_rms = lax.rsqrt(jnp.mean(xf * xf, axis=1, keepdims=True) + 1e-05)
    normed = (xf * inv_rms * norm_gain).astype(jnp.bfloat16)
    grad_pre = rope_back(key_cotangent, positions)
    grad_all = lax.all_gather(grad_pre, "seq", axis=0, tiled=True)
    split_normed = (
        normed.reshape(tok_rows, row_blocks, groups, part_rows)
        .transpose(0, 2, 1, 3)
        .reshape(tok_rows, groups, row_blocks * part_rows)
    )
    received = lax.all_to_all(split_normed, "seq", split_axis=1, concat_axis=0, tiled=True)
    normed_rows = received.reshape(groups * tok_rows, row_blocks, part_rows)
    divisor = math.sqrt(SEQ_LEN * lax.axis_size("dp"))
    count = row_blocks // lax.axis_size("dp") * lax.axis_size("dp")
    slab = normed_rows.reshape(groups * tok_rows, count * part_rows)
    product = lax.dot_general(
        slab, grad_all, (((0,), (0,)), ((), ())), preferred_element_type=jnp.float32
    )
    shaped = (
        product.reshape(count, part_rows, col_blocks, BLK)
        .transpose(0, 2, 1, 3)
        .reshape(count, col_blocks, part_rows * BLK)
    )
    cols = kept_cols
    counts = kept_count
    picked = jnp.take_along_axis(shaped, cols[:, :, None], axis=1)
    live = lax.broadcasted_iota(jnp.int32, (count, MOSTR), 1) < counts[:, None]
    block_grad = lax.psum_scatter(
        jnp.where(live[:, :, None], picked / divisor, jnp.float32(0.0)),
        "dp",
        scatter_dimension=0,
        tiled=True,
    )
    piece = lax.all_gather(key_blocks, "dp", axis=0, tiled=True)
    cols = kept_cols
    counts = kept_count
    dense = densify(piece, cols, counts, BLK)
    normed_grad = lax.dot_general(
        grad_pre, dense, (((1,), (1,)), ((), ())), preferred_element_type=jnp.float32
    )
    scaled = norm_gain * normed_grad
    grads = inv_rms * scaled - inv_rms**3 * xf * jnp.mean(scaled * xf, axis=1, keepdims=True)
    return (grads.astype(jnp.bfloat16), block_grad)


def solution(mesh):
    placed = (
        P(("dp", "seq"), None),
        P(),
        P(("dp", "seq"), None),
        P(("dp", "seq")),
        P(),
        P(),
        P("dp", None, None),
    )
    return jax.shard_map(
        shards,
        mesh=mesh,
        in_specs=placed,
        out_specs=(P(("dp", "seq"), None), P("dp", None, "seq")),
        check_vma=False,
    )
```

profile of v0, /device:TPU:2, one launch (start us, length us, event | category | flops | bytes accessed | tf_op | source)
XLA Modules:
  0.0 578.3 jit_solution(3472981876656661758)
XLA Ops:
  7.2 0.0 all-gather.3.cloned.1.call-start
  7.2 1.6 copy.31
  8.8 0.0 all-gather.3.cloned.1.call-update
  8.8 0.0 all-gather.5.cloned.1.call-start
  8.9 0.7 convert_element_type.35
  9.6 1.1 copy.29
  10.7 0.2 multiply_cosine_fusion
  10.9 0.1 multiply_add_fusion
  11.0 0.7 maximum_convert_fusion
  11.8 0.0 all-gather.5.cloned.1.call-update
  11.8 0.7 iota_compare_fusion.1
  12.5 0.8 copy.30
  13.3 102.3 %all-gather.3.cloned.1.call-done = bf16[128,6,4096]{2,1,0:T(8,128)(2,1)} async-done(((bf16[2,6,4096]{2,1,0:T(8,128)(2,1)}), bf16[128,6,4096]{2,1,0:T(8,128)(2,1)}) %all-gather.3.cloned.1.call-update) | async-done | bytes 6291472 | tf_op jit(solution)/shard_map/all_gather | solution.py:81
  115.7 14.6 %fusion.9 = bf16[128,16,4096]{2,1,0:T(8,128)(2,1)} fusion(bf16[128,6,4096]{2,1,0:T(8,128)(2,1)} %all-gather.3.cloned.1.call-done, s32[128,6]{1,0:T(8,128)S(1)} %copy.30, pred[128,6]{1,0:T(8,128)(4,1)S(1)} %iota_compare_fusion.1), kind=kOutput, calls=%fused_computation.20 | convolution fusion | flops 100687872 | bytes 23072512 | tf_op jit(solution)/shard_map/dot_general | solution.py:35
  130.2 22.6 %copy.32 = bf16[128,16,4096]{0,2,1:T(8,128)(2,1)} copy(bf16[128,16,4096]{2,1,0:T(8,128)(2,1)} %fusion.9) | data formatting | bytes 33554432 | tf_op jit(solution)/shard_map/dot_general | solution.py:35
  152.8 46.0 %copy.33 = bf16[128,64,16,64]{3,2,1,0:T(8,128)(2,1)} copy(bf16[128,64,16,64]{0,3,1,2:T(8,128)(2,1)} %bitcast.39) | data formatting | bytes 33554432 | tf_op jit(solution)/shard_map/transpose | solution.py:38
  198.8 0.0 copy-start
  198.8 0.0 copy-start.1
  198.8 0.0 copy-start.2
  198.8 44.3 %reshape.139 = bf16[8192,1024]{1,0:T(8,128)(2,1)} reshape(bf16[128,64,16,64]{3,2,1,0:T(8,128)(2,1)} %copy.33) | data formatting | bytes 33554432 | tf_op jit(solution)/shard_map/reshape | solution.py:39
  243.1 0.0 copy-done
  243.1 0.0 copy-done.1
  243.1 0.0 copy-done.2
  243.1 13.6 %fusion = (f32[128]{0:T(128)S(1)}, f32[128]{0:T(128)S(1)}, f32[128,8192]{1,0:T(8,128)}) fusion(bf16[128,8192]{1,0:T(8,128)(2,1)S(1)} %copy-done, bf16[128,1024]{0,1:T(8,128)(2,1)S(1)} %bitcast.46, bf16[8192,1024]{1,0:T(8,128)(2,1)} %reshape.139, f32[8192]{0:T(1024)S(1)} %copy-done.2), kind=kOutput, calls=%fused_computation.6 | convolution fusion | flops 2153775104 | bytes 23364608 | tf_op jit(solution)/shard_map/dot_general | solution.py:85
  256.7 6.0 %fusion.6 = (bf16[128,8192]{1,0:T(8,128)(2,1)}, bf16[128,8192]{1,0:T(8,128)(2,1)}) fusion(bf16[128,8192]{1,0:T(8,128)(2,1)S(1)} %copy-done, f32[8192]{0:T(1024)S(1)} %copy-done.2, f32[128]{0:T(128)S(1)} %get-tuple-element.14, f32[128]{0:T(128)S(1)} %get-tuple-element.17, f32[128]{0:T(128)S(1)} %get-tuple-element.15, f32[128,8192]{1,0:T(8,128)} %get-tuple-element.16), kind=kLoop, calls=%fused_computation.12 | loop fusion | flops 9437184 | bytes 10520064 | tf_op jit(solution)/shard_map/convert_element_type | solution.py:50
  262.8 3.4 copy.35
  266.2 0.0 copy-start.3
  266.2 1.7 copy.50
  267.9 4.9 all-to-all-start
  272.8 0.0 reduce-scatter.2.cloned.1.call-start
  272.8 0.0 copy-done.3
  272.8 0.1 copy.41
  272.9 0.1 reshape.145
  273.0 0.1 copy.34
  273.2 25.3 %all-to-all-done = bf16[128,8,1024]{0,2,1:T(8,128)(2,1)S(1)} async-done(((bf16[128,8,1024]{0,2,1:T(8,128)(2,1)}), bf16[128,8,1024]{0,2,1:T(8,128)(2,1)S(1)}, u32[]{:S(2)}, u32[]{:S(2)}) %all-to-all-start) | async-done | bytes 2097184 | tf_op jit(solution)/shard_map/all_to_all | solution.py:58
  298.5 2.6 copy.37
  301.1 2.9 copy.38
  304.0 0.0 all-gather.5.cloned.1.call-done
  304.0 4.9 convolution_bitcast_fusion
  308.9 2.3 copy.40
  311.2 5.5 copy.42
  316.7 7.5 %gather_fusion = f32[768,512]{1,0:T(8,128)S(1)} fusion(f32[128,16,512]{2,1,0:T(8,128)} %copy.42, s32[768]{0:T(1024)S(1)} %reshape.145), kind=kCustom, calls=%fused_computation | custom fusion | bytes 3151872 | tf_op jit(solution)/shard_map/jit(take_along_axis)/gather | solution.py:73
  324.2 1.5 reshape.148
  325.7 2.8 multiply_select_fusion
  328.5 0.0 reduce-scatter.2.cloned.1.call-update
  328.5 241.8 %reduce-scatter.2.cloned.1.call-done = f32[2,6,512]{2,1,0:T(8,128)} async-done(((f32[128,6,512]{2,1,0:T(8,128)}), f32[2,6,512]{2,1,0:T(8,128)}) %reduce-scatter.2.cloned.1.call-update) | async-done | bytes 24592 | tf_op jit(solution)/shard_map/reduce_scatter | solution.py:75
  570.4 1.4 copy.43
  (5 shorter events, 0.1 us)
Async XLA Ops:
  7.2 108.5 %all-gather.3.cloned.1.call-start = ((), (), s32[]{:S(2)}) async-start(), calls=%async_computation.2 | async-start | bytes 8519680 | tf_op jit(solution)/shard_map/all_gather | solution.py:81
  8.8 295.1 %all-gather.5.cloned.1.call-start = ((), (), s32[]{:S(2)}) async-start(), calls=%async_computation.3 | async-start | bytes 2359296 | tf_op jit(solution)/shard_map/all_gather | solution.py:52
  198.8 44.3 %copy-start = (bf16[128,8192]{1,0:T(8,128)(2,1)S(1)}, bf16[128,8192]{1,0:T(8,128)(2,1)}, u32[]{:S(2)}) copy-start(bf16[128,8192]{1,0:T(8,128)(2,1)} %param.7) | copy-start | bytes 6291460
  198.8 44.3 %copy-start.1 = (bf16[128,8,2,64]{0,3,2,1:T(8,128)(2,1)S(1)}, bf16[128,8,2,64]{0,3,2,1:T(8,128)(2,1)}, u32[]{:S(2)}) copy-start(bf16[128,8,2,64]{0,3,2,1:T(8,128)(2,1)} %maximum_convert_fusion) | copy-start | bytes 786436
  198.8 44.3 %copy-start.2 = (f32[8192]{0:T(1024)S(1)}, f32[8192]{0:T(1024)}, u32[]{:S(2)}) copy-start(f32[8192]{0:T(1024)} %param.8) | copy-start | bytes 98308
  266.2 6.6 %copy-start.3 = (s32[128,6]{0,1:T(8,128)S(1)}, s32[128,6]{0,1:T(8,128)}, u32[]{:S(2)}) copy-start(s32[128,6]{0,1:T(8,128)} %param.11) | copy-start | bytes 9220
  267.9 30.6 %all-to-all-start = ((bf16[128,8,1024]{0,2,1:T(8,128)(2,1)}), bf16[128,8,1024]{0,2,1:T(8,128)(2,1)S(1)}, u32[]{:S(2)}, u32[]{:S(2)}) async-start(bf16[128,8,1024]{0,2,1:T(8,128)(2,1)} %bitcast.42), calls=%async_computation | async-start | bytes 4194304 | tf_op jit(solution)/shard_map/all_to_all | solution.py:58
  272.8 297.6 %reduce-scatter.2.cloned.1.call-start = ((), (), s32[]{:S(2)}) async-start(), calls=%async_computation.4 | async-start | bytes 2129920 | tf_op jit(solution)/shard_map/reduce_scatter | solution.py:75
Sparse Core Ops, SparseCore 0:
  11.6 103.9 all-gather.2
  117.8 30.1 all-gather.4
  328.7 241.6 reduce-scatter.1
where the time goes:
time: 582 us; the launch traced here: 578 us
  waiting for transfers between devices  370 us (64%)
  local copies, waits for them, and re-layouts  146 us (25%)
  matrix products  33.1 us (6%)
  between operations  13.9 us (2%)
  other arithmetic  11.3 us (2%)
    reduce_scatter x1, waiting for transfers between devices, shards(): lax.psum_scatter(jnp.where(live[:, :, None], picked / divisor, jnp.float3...  242 us
    all_gather x1, waiting for transfers between devices, shards(): piece = lax.all_gather(key_blocks, 'dp', axis=0, tiled=True)  102 us
    transpose x1, local copies, waits for them, and re-layouts, densify(): placed.reshape(count_rows, col_blocks, rows, BLK).transpose(0, 2, 1, 3)  46 us
    reshape x1, local copies, waits for them, and re-layouts, densify(): return dense.reshape(count_rows * rows, KVW)  44.3 us
    all_to_all x1, waiting for transfers between devices, shards(): lax.all_to_all(split_normed, 'seq', split_axis=1, concat_axis=0, tiled=True)  25.3 us
    dot_general x1, local copies, waits for them, and re-layouts, densify(): lax.dot_general(onehot, blocks, (((1,), (1,)), ((0,), (0,))), preferred_e...  22.6 us
    dot_general x1, matrix products, densify(): lax.dot_general(onehot, blocks, (((1,), (1,)), ((0,), (0,))), preferred_e...  14.6 us
    dot_general x1, matrix products, shards(): lax.dot_general(grad_pre, dense, (((1,), (1,)), ((), ())), preferred_elem...  13.6 us
  transfers between devices with their start and end apart: 4, of which 3 were waited for; matrix products, arithmetic and copies ran while one was open for 28% of the time, Pallas kernels for 0%

commit v1 on v0

--- a/solution.py
+++ b/solution.py
@@ -78,7 +78,9 @@
         scatter_dimension=0,
         tiled=True,
     )
-    piece = lax.all_gather(key_blocks, "dp", axis=0, tiled=True)
+    piece = jnp.concatenate(
+        lax.all_to_all(jnp.stack([key_blocks] * lax.axis_size("dp")), "dp", 0, 0), axis=0
+    )
     cols = kept_cols
     counts = kept_count
     dense = densify(piece, cols, counts, BLK)

time: 582 us -> 707 us (1.21)
  waiting for transfers between devices: 370 us -> 470 us
  starting transfers between devices: 4.95 us -> 21.8 us
  local copies, waits for them, and re-layouts: 146 us -> 157 us
    all_to_all x0 -> x1, waiting for transfers between devices: none -> 167 us  [shards(): lax.all_to_all(jnp.stack([key_blocks] * lax.axis_size('dp')), 'dp', 0, 0)]
    all_gather x1 -> x0, waiting for transfers between devices: 102 us -> none  [shards(): piece = lax.all_gather(key_blocks, 'dp', axis=0, tiled=True)]
    reduce_scatter x1, waiting for transfers between devices: 242 us -> 277 us  [shards(): lax.psum_scatter(jnp.where(live[:, :, None], picked / divisor, jnp.float3...]
    all_to_all x0 -> x1, starting transfers between devices: none -> 17 us  [shards(): lax.all_to_all(jnp.stack([key_blocks] * lax.axis_size('dp')), 'dp', 0, 0)]
    all_to_all x0 -> x1, local copies, waits for them, and re-layouts: none -> 10.2 us  [shards(): lax.all_to_all(jnp.stack([key_blocks] * lax.axis_size('dp')), 'dp', 0, 0)]
  transfers between devices with their start and end apart: 4 -> 4, of which waited for: 3 -> 3; matrix products, arithmetic and copies ran while one was open for 28% -> 24% of each run, Pallas kernels for 0% -> 0%
where the time goes in v1:
time: 707 us; the launch traced here: 703 us
  waiting for transfers between devices  470 us (66%)
  local copies, waits for them, and re-layouts  157 us (22%)
  matrix products  30.2 us (4%)
  starting transfers between devices  21.8 us (3%)
  between operations  14.2 us (2%)
  other arithmetic  9.99 us (1%)
    reduce_scatter x1, waiting for transfers between devices, shards(): lax.psum_scatter(jnp.where(live[:, :, None], picked / divisor, jnp.float3...  277 us
    all_to_all x1, waiting for transfers between devices, shards(): lax.all_to_all(jnp.stack([key_blocks] * lax.axis_size('dp')), 'dp', 0, 0)  167 us
    transpose x1, local copies, waits for them, and re-layouts, densify(): placed.reshape(count_rows, col_blocks, rows, BLK).transpose(0, 2, 1, 3)  46 us
    reshape x1, local copies, waits for them, and re-layouts, densify(): return dense.reshape(count_rows * rows, KVW)  44.3 us
    all_to_all x1, waiting for transfers between devices, shards(): lax.all_to_all(split_normed, 'seq', split_axis=1, concat_axis=0, tiled=True)  25.3 us
    dot_general x1, local copies, waits for them, and re-layouts, densify(): lax.dot_general(onehot, blocks, (((1,), (1,)), ((0,), (0,))), preferred_e...  22.5 us
    all_to_all x1, starting transfers between devices, shards(): lax.all_to_all(jnp.stack([key_blocks] * lax.axis_size('dp')), 'dp', 0, 0)  17 us
  transfers between devices with their start and end apart: 4, of which 3 were waited for; matrix products, arithmetic and copies ran while one was open for 24% of the time, Pallas kernels for 0%

profile of v1, /device:TPU:2, one launch (start us, length us, event | category | flops | bytes accessed | tf_op | source)
XLA Modules:
  0.0 703.1 jit_solution(5472048976500251336)
XLA Ops:
  7.2 5.1 stack.5
  12.2 0.0 copy-start.6
  12.2 0.0 copy-start.2
  12.2 0.0 copy-start.4
  12.2 0.0 copy-start.5
  12.3 17.0 %all-to-all-start = ((bf16[64,2,6,4096]{3,1,2,0:T(2,128)(2,1)}), bf16[64,2,6,4096]{3,1,2,0:T(2,128)(2,1)}, u32[]{:S(2)}, u32[]{:S(2)}) async-start(bf16[64,2,6,4096]{3,1,2,0:T(2,128)(2,1)} %stack.5), calls=%async_computation | async-start | bytes 12582912 | tf_op jit(solution)/shard_map/all_to_all | solution.py:82
  29.2 0.0 all-gather.2.cloned.1.call-start
  29.3 0.0 copy-done.6
  29.3 0.0 copy-done.2
  29.3 0.2 copy.29
  29.5 0.2 multiply_cosine_fusion
  29.7 0.1 multiply_add_fusion
  29.8 0.7 maximum_convert_fusion
  30.6 0.0 all-gather.2.cloned.1.call-update
  30.6 0.0 copy-done.4
  30.6 0.1 copy.30
  30.7 0.0 copy-done.5
  30.7 0.1 iota_compare_fusion.1
  30.8 167.3 %all-to-all-done = bf16[64,2,6,4096]{3,1,2,0:T(2,128)(2,1)} async-done(((bf16[64,2,6,4096]{3,1,2,0:T(2,128)(2,1)}), bf16[64,2,6,4096]{3,1,2,0:T(2,128)(2,1)}, u32[]{:S(2)}, u32[]{:S(2)}) %all-to-all-start) | async-done | bytes 6291488 | tf_op jit(solution)/shard_map/all_to_all | solution.py:82
  198.1 10.2 %copy.31 = bf16[64,2,6,4096]{3,2,1,0:T(8,128)(2,1)S(1)} copy(bf16[64,2,6,4096]{3,1,2,0:T(2,128)(2,1)} %all-to-all-done) | data formatting | bytes 12582912 | tf_op jit(solution)/shard_map/all_to_all | solution.py:82
  208.3 11.7 %fusion.9 = bf16[128,16,4096]{2,1,0:T(8,128)(2,1)} fusion(bf16[128,6,4096]{2,1,0:T(8,128)(2,1)S(1)} %bitcast.41, s32[128,6]{1,0:T(8,128)S(1)} %copy.30, pred[128,6]{1,0:T(8,128)(4,1)S(1)} %iota_compare_fusion.1), kind=kOutput, calls=%fused_computation.20 | convolution fusion | flops 100687872 | bytes 23072512 | tf_op jit(solution)/shard_map/dot_general | solution.py:35
  220.0 22.5 %copy.32 = bf16[128,16,4096]{0,2,1:T(8,128)(2,1)} copy(bf16[128,16,4096]{2,1,0:T(8,128)(2,1)} %fusion.9) | data formatting | bytes 33554432 | tf_op jit(solution)/shard_map/dot_general | solution.py:35
  242.5 46.0 %copy.33 = bf16[128,64,16,64]{3,2,1,0:T(8,128)(2,1)} copy(bf16[128,64,16,64]{0,3,1,2:T(8,128)(2,1)} %bitcast.40) | data formatting | bytes 33554432 | tf_op jit(solution)/shard_map/transpose | solution.py:38
  288.4 0.0 copy-start
  288.4 0.0 copy-start.1
  288.4 0.0 copy-start.3
  288.4 44.3 %reshape.145 = bf16[8192,1024]{1,0:T(8,128)(2,1)} reshape(bf16[128,64,16,64]{3,2,1,0:T(8,128)(2,1)} %copy.33) | data formatting | bytes 33554432 | tf_op jit(solution)/shard_map/reshape | solution.py:39
  332.7 0.0 copy-done
  332.7 0.0 copy-done.1
  332.7 0.0 copy-done.3
  332.7 13.6 %fusion = (f32[128]{0:T(128)S(1)}, f32[128]{0:T(128)S(1)}, f32[128,8192]{1,0:T(8,128)}) fusion(bf16[128,8192]{1,0:T(8,128)(2,1)S(1)} %copy-done, bf16[128,1024]{0,1:T(8,128)(2,1)S(1)} %bitcast.48, bf16[8192,1024]{1,0:T(8,128)(2,1)} %reshape.145, f32[8192]{0:T(1024)S(1)} %copy-done.3), kind=kOutput, calls=%fused_computation.6 | convolution fusion | flops 2153775104 | bytes 23364608 | tf_op jit(solution)/shard_map/dot_general | solution.py:87
  346.4 6.0 fusion.6
  352.4 3.2 copy.35
  355.6 1.7 copy.50
  357.3 4.8 all-to-all-start.1
  362.2 0.0 reduce-scatter.2.cloned.1.call-start
  362.2 0.1 copy.41
  362.3 0.1 reshape.151
  362.4 0.1 copy.34
  362.6 25.3 %all-to-all-done.1 = bf16[128,8,1024]{0,2,1:T(8,128)(2,1)S(1)} async-done(((bf16[128,8,1024]{0,2,1:T(8,128)(2,1)}), bf16[128,8,1024]{0,2,1:T(8,128)(2,1)S(1)}, u32[]{:S(2)}, u32[]{:S(2)}) %all-to-all-start.1) | async-done | bytes 2097184 | tf_op jit(solution)/shard_map/all_to_all | solution.py:58
  387.9 2.6 copy.37
  390.5 2.9 copy.38
  393.4 0.0 all-gather.2.cloned.1.call-done
  393.4 4.9 convolution_bitcast_fusion
  398.3 2.3 copy.40
  400.6 5.5 copy.42
  406.1 7.5 %gather_fusion = f32[768,512]{1,0:T(8,128)S(1)} fusion(f32[128,16,512]{2,1,0:T(8,128)} %copy.42, s32[768]{0:T(1024)S(1)} %reshape.151), kind=kCustom, calls=%fused_computation | custom fusion | bytes 3151872 | tf_op jit(solution)/shard_map/jit(take_along_axis)/gather | solution.py:73
  413.6 1.5 reshape.154
  415.1 2.8 multiply_select_fusion
  417.9 0.0 reduce-scatter.2.cloned.1.call-update
  417.9 277.0 %reduce-scatter.2.cloned.1.call-done = f32[2,6,512]{2,1,0:T(8,128)} async-done(((f32[128,6,512]{2,1,0:T(8,128)}), f32[2,6,512]{2,1,0:T(8,128)}) %reduce-scatter.2.cloned.1.call-update) | async-done | bytes 24592 | tf_op jit(solution)/shard_map/reduce_scatter | solution.py:75
  694.9 1.4 copy.43
  (6 shorter events, 0.1 us)
Async XLA Ops:
  12.2 17.0 %copy-start.6 = (s32[128]{0:T(128)S(1)}, s32[128]{0:T(128)}, u32[]{:S(2)}) copy-start(s32[128]{0:T(128)} %param.10) | copy-start | bytes 1540
  12.2 17.1 %copy-start.2 = (bf16[128,1024]{1,0:T(8,128)(2,1)S(1)}, bf16[128,1024]{1,0:T(8,128)(2,1)}, u32[]{:S(2)}) copy-start(bf16[128,1024]{1,0:T(8,128)(2,1)} %param.9) | copy-start | bytes 786436
  12.2 18.4 %copy-start.4 = (s32[128,6]{0,1:T(8,128)S(1)}, s32[128,6]{0,1:T(8,128)}, u32[]{:S(2)}) copy-start(s32[128,6]{0,1:T(8,128)} %param.11) | copy-start | bytes 9220
  12.2 18.5 %copy-start.5 = (s32[128]{0:T(128)S(1)}, s32[128]{0:T(128)}, u32[]{:S(2)}) copy-start(s32[128]{0:T(128)} %param.12) | copy-start | bytes 1540
  12.3 185.9 %all-to-all-start = ((bf16[64,2,6,4096]{3,1,2,0:T(2,128)(2,1)}), bf16[64,2,6,4096]{3,1,2,0:T(2,128)(2,1)}, u32[]{:S(2)}, u32[]{:S(2)}) async-start(bf16[64,2,6,4096]{3,1,2,0:T(2,128)(2,1)} %stack.5), calls=%async_computation | async-start | bytes 12582912 | tf_op jit(solution)/shard_map/all_to_all | solution.py:82
  29.2 364.2 %all-gather.2.cloned.1.call-start = ((), (), s32[]{:S(2)}) async-start(), calls=%async_computation.3 | async-start | bytes 2359296 | tf_op jit(solution)/shard_map/all_gather | solution.py:52
  288.4 44.3 %copy-start = (bf16[128,8192]{1,0:T(8,128)(2,1)S(1)}, bf16[128,8192]{1,0:T(8,128)(2,1)}, u32[]{:S(2)}) copy-start(bf16[128,8192]{1,0:T(8,128)(2,1)} %param.7) | copy-start | bytes 6291460
  288.4 44.3 %copy-start.1 = (bf16[128,8,2,64]{0,3,2,1:T(8,128)(2,1)S(1)}, bf16[128,8,2,64]{0,3,2,1:T(8,128)(2,1)}, u32[]{:S(2)}) copy-start(bf16[128,8,2,64]{0,3,2,1:T(8,128)(2,1)} %maximum_convert_fusion) | copy-start | bytes 786436
  288.4 44.3 %copy-start.3 = (f32[8192]{0:T(1024)S(1)}, f32[8192]{0:T(1024)}, u32[]{:S(2)}) copy-start(f32[8192]{0:T(1024)} %param.8) | copy-start | bytes 98308
  357.3 30.6 %all-to-all-start.1 = ((bf16[128,8,1024]{0,2,1:T(8,128)(2,1)}), bf16[128,8,1024]{0,2,1:T(8,128)(2,1)S(1)}, u32[]{:S(2)}, u32[]{:S(2)}) async-start(bf16[128,8,1024]{0,2,1:T(8,128)(2,1)} %bitcast.44), calls=%async_computation.1 | async-start | bytes 4194304 | tf_op jit(solution)/shard_map/all_to_all | solution.py:58
  362.2 332.7 %reduce-scatter.2.cloned.1.call-start = ((), (), s32[]{:S(2)}) async-start(), calls=%async_computation.4 | async-start | bytes 2129920 | tf_op jit(solution)/shard_map/reduce_scatter | solution.py:75
Sparse Core Ops, SparseCore 0:
  32.2 32.7 all-gather.1
  418.1 276.7 reduce-scatter.1
